TPU v7x, 512 devices: a whole 4x8x8 slice. The times are simulated.
512 devices in a mesh: grp: 16 (over y, core), dom: 32 (over x, z).
Axes of the slice: x: 4, y: 8, z: 8, core: 2. Of those that a mesh axis runs over, the one named last changes fastest.
Arguments:
- owned_blips: bfloat16 [2048, 32768], P(('grp', 'dom')), may hold values from -6 to 6
- potential: float32 [32, 512, 1024], P('dom', 'grp'), may hold values from -5 to 5
- slot_owner: int32 [12288, 1], P(('grp', 'dom')), may hold values from 0 to 31; in each aligned block of 24 rows (0 to 23, 24 to 47, ...) at most 2 rows name the same one
- slot_row: int32 [12288], P(('grp', 'dom')), may hold values from 0 to 3
- slot_offset: int32 [12288], P(('grp', 'dom')), may hold values from 0 to 31
Outputs:
- blip_gradient: float32 [2048, 32768], P(('grp', 'dom'))
- hamiltonian: float32 [2048, 128], P(('grp', 'dom'))
Inputs may be any that keep to these rules, and one draw needn't show every extreme that they name: `slot_owner`: among the 24 pieces of one device at most 2 name the same owner.
All inputs are finite; a program needn't handle non-finite values.
Results may differ from a plain program's by a relative error of at most 0.012.
The roundings to bfloat16 on the way count: a program that leaves them out, or rounds other values in their place, can miss the bound.
Values may be sent and summed in bfloat16 or wider, within the bound.
No kernel may reach another device: no remote copies, remote signals or barrier semaphores. Data moves between devices by JAX's collectives and lax.ppermute only.
A program may use at most 128 MiB of HBM per device.

v0:
```python
import jax
import jax.numpy as jnp
from jax import lax
from jax.sharding import PartitionSpec as P

NB = 32


def passed_along(block, axis, distance):
    devices = range(lax.axis_size(axis))
    route = [((i - distance) % len(devices), i) for i in devices]
    return lax.ppermute(block, axis, route)


def spline_tables():
    cells_line = jnp.arange(NB, dtype=jnp.int32)
    offset = cells_line[:, None] - cells_line[None, :]
    spline = jnp.where(
        offset == 0, 2.0 / 3.0, jnp.where(jnp.abs(offset) == 1, 1.0 / 6.0, 0.0)
    ).astype(jnp.float32)
    second = jnp.where(offset == 0, -2.0, jnp.where(jnp.abs(offset) == 1, 1.0, 0.0)).astype(
        jnp.float32
    )
    plane_value = jnp.einsum("ac,bd->abcd", spline, spline).reshape(NB * NB, NB * NB)
    plane_curve = (
        jnp.einsum("ac,bd->abcd", second, spline) + jnp.einsum("ac,bd->abcd", spline, second)
    ).reshape(NB * NB, NB * NB)
    return (
        spline.astype(jnp.bfloat16),
        second.astype(jnp.bfloat16),
        plane_value.astype(jnp.bfloat16),
        plane_curve.astype(jnp.bfloat16),
    )


def on_device(owned_blips, potential, slot_owner, slot_row, slot_offset):
    spline, second, plane_value, plane_curve = spline_tables()
    domain_count = lax.axis_size("dom")
    slot_count = slot_row.shape[0]
    owned_count = owned_blips.shape[0]
    cell_count = owned_blips.shape[1]
    plane_cells = NB * NB
    capacity = max(2, -(-slot_count // domain_count))
    group_size = domain_count * owned_count
    owner_of = slot_owner[:, 0]
    target = owner_of * owned_count + slot_row
    owner_hot = (owner_of[:, None] == jnp.arange(domain_count, dtype=jnp.int32)[None, :]).astype(
        jnp.int32
    )
    position = jnp.sum(jnp.cumsum(owner_hot, axis=0) * owner_hot, axis=1) - 1
    place_slot = owner_of * capacity + position
    place_hot = place_slot[None, :] == jnp.arange(domain_count * capacity, dtype=jnp.int32)[:, None]
    asked_rows = jnp.sum(jnp.where(place_hot, slot_row[None, :], 0), axis=1) + owned_count * (
        1 - jnp.sum(place_hot.astype(jnp.int32), axis=1)
    )
    place_low = place_hot.astype(jnp.bfloat16)
    gathered_rows = lax.all_gather(owned_blips, "dom", axis=0, tiled=True)
    chosen = (
        target[:, None] == jnp.arange(gathered_rows.shape[0], dtype=jnp.int32)[None, :]
    ).astype(jnp.bfloat16)
    slot_blips = jnp.dot(chosen, gathered_rows, preferred_element_type=jnp.float32).astype(
        jnp.bfloat16
    )
    upper_cells = passed_along(potential, "grp", -1)
    extended = jnp.concatenate([potential[0], upper_cells[0]], axis=0)

    def cut_window(first_row):
        return lax.dynamic_slice_in_dim(extended, first_row, NB, 0)

    window = jax.vmap(cut_window)(slot_offset)
    layered = slot_blips.reshape(slot_count, NB, plane_cells)
    y_value = jnp.einsum("ya,sab->syb", spline, layered, preferred_element_type=jnp.float32).astype(
        jnp.bfloat16
    )
    y_curve = jnp.einsum("ya,sab->syb", second, layered, preferred_element_type=jnp.float32).astype(
        jnp.bfloat16
    )
    flat_value = y_value.reshape(-1, plane_cells)
    values_grid = jnp.dot(flat_value, plane_value, preferred_element_type=jnp.float32)
    laplace = jnp.dot(
        y_curve.reshape(-1, plane_cells), plane_value, preferred_element_type=jnp.float32
    ) + jnp.dot(flat_value, plane_curve, preferred_element_type=jnp.float32)
    applied = (-0.5 * laplace + window.reshape(-1, plane_cells) * values_grid).astype(jnp.bfloat16)
    values_low = values_grid.astype(jnp.bfloat16)
    back_plane = jnp.dot(applied, plane_value, preferred_element_type=jnp.float32).astype(
        jnp.bfloat16
    )
    gradient_piece = jnp.einsum(
        "ay,sab->syb",
        spline,
        back_plane.reshape(slot_count, NB, plane_cells),
        preferred_element_type=jnp.float32,
    ).astype(jnp.bfloat16)
    intersection = lax.dot_general(
        values_low.reshape(slot_count, cell_count),
        applied.reshape(slot_count, cell_count),
        (((1,), (1,)), ((), ())),
        preferred_element_type=jnp.float32,
    ) / float(cell_count)
    select_full = (target[:, None] == jnp.arange(group_size, dtype=jnp.int32)[None, :]).astype(
        jnp.float32
    )
    weighted = jnp.dot(intersection, select_full, precision=lax.Precision.HIGHEST)
    place_f32 = place_hot.astype(jnp.float32)
    send_ham = jnp.concatenate(
        [
            jnp.dot(place_f32, weighted, precision=lax.Precision.HIGHEST),
            asked_rows.astype(jnp.float32)[:, None],
        ],
        axis=1,
    ).reshape(domain_count, capacity, group_size + 1)
    got_ham = lax.all_to_all(send_ham, "dom", split_axis=0, concat_axis=0, tiled=True).reshape(
        domain_count * capacity, group_size + 1
    )
    got_rows = got_ham[:, group_size]
    send_grad = jnp.dot(
        place_low,
        gradient_piece.reshape(slot_count, cell_count),
        preferred_element_type=jnp.bfloat16,
    ).reshape(domain_count, capacity, cell_count)
    got_grad = lax.all_to_all(send_grad, "dom", split_axis=0, concat_axis=0, tiled=True)
    row_hot = got_rows[None, :] == jnp.arange(owned_count, dtype=jnp.float32)[:, None]
    hamilton = jnp.dot(
        row_hot.astype(jnp.float32), got_ham[:, :group_size], precision=lax.Precision.HIGHEST
    )
    gradient = jnp.dot(
        row_hot.astype(jnp.bfloat16),
        got_grad.reshape(-1, cell_count),
        preferred_element_type=jnp.float32,
    )
    return (gradient, hamilton)


def solution(mesh):
    placed = (
        P(("grp", "dom"), None),
        P("dom", "grp", None),
        P(("grp", "dom"), None),
        P(("grp", "dom")),
        P(("grp", "dom")),
    )
    return jax.shard_map(
        on_device,
        mesh=mesh,
        in_specs=placed,
        out_specs=(P(("grp", "dom"), None), P(("grp", "dom"), None)),
        check_vma=False,
    )
```

profile of v0, /device:TPU:8, one launch (start us, length us, event | category | flops | bytes accessed | tf_op | source)
XLA Modules:
  0.0 299.2 jit_solution(602557687519509434)
XLA Ops:
  11.2 7.6 %fusion.1 = (bf16[32,32,32,32]{3,2,1,0:T(8,128)(2,1)}, bf16[32,32,32,32]{3,2,1,0:T(8,128)(2,1)}) fusion(f32[32,32]{1,0:T(8,128)S(1)} %copy.43, f32[32,32]{1,0:T(8,128)S(1)} %copy.40), kind=kLoop, calls=%fused_computation.6 | loop fusion | flops 6291456 | bytes 4202496 | tf_op jit(solution)/shard_map/convert_element_type | solution.py:32
  18.7 12.4 %convert_element_type.92 = bf16[1024,1024]{1,0:T(8,128)(2,1)} reshape(bf16[32,32,32,32]{3,2,1,0:T(8,128)(2,1)} %get-tuple-element.21) | data formatting | bytes 4194304 | tf_op jit(solution)/shard_map/convert_element_type | solution.py:31
  31.1 11.4 %convert_element_type.99 = bf16[1024,1024]{1,0:T(8,128)(2,1)S(1)} reshape(bf16[32,32,32,32]{3,2,1,0:T(8,128)(2,1)} %get-tuple-element.20) | data formatting | bytes 4194304 | tf_op jit(solution)/shard_map/convert_element_type | solution.py:32
  42.8 45.6 %while.1 = (s32[]{:T(128)}, f32[64,1024]{1,0:T(8,128)S(1)}, s32[24,2]{0,1:T(2,128)S(1)}, f32[24,32,1024]{2,1,0:T(8,128)}, s32[]{:T(128)}) while((s32[]{:T(128)}, f32[64,1024]{1,0:T(8,128)S(1)}, s32[24,2]{0,1:T(2,128)S(1)}, f32[24,32,1024]{2,1,0:T(8,128)}, s32[]{:T(128)}) %tuple.24), condition=%wide.while_cond, body=%wide.while_body.sunk | while | flops 2 | bytes 263257 | solution.py:68
  52.9 1.3 bitcast_dynamic-update-slice_fusion.2
  54.8 1.3 bitcast_dynamic-update-slice_fusion.2
  58.5 1.3 bitcast_dynamic-update-slice_fusion.2
  64.2 1.3 bitcast_dynamic-update-slice_fusion.2
  66.1 1.3 bitcast_dynamic-update-slice_fusion.2
  69.9 1.3 bitcast_dynamic-update-slice_fusion.2
  75.6 1.3 bitcast_dynamic-update-slice_fusion.2
  77.5 1.3 bitcast_dynamic-update-slice_fusion.2
  81.3 1.3 bitcast_dynamic-update-slice_fusion.2
  85.1 1.3 bitcast_dynamic-update-slice_fusion.2
  87.0 1.3 bitcast_dynamic-update-slice_fusion.2
  88.4 31.4 %all-gather.3.cloned.1.call-done = bf16[32,4,32768]{2,1,0:T(4,128)(2,1)} async-done(((bf16[1,4,32768]{2,1,0:T(4,128)(2,1)}), bf16[32,4,32768]{2,1,0:T(4,128)(2,1)}) %all-gather.3.cloned.1.call-update) | async-done | bytes 8388624 | tf_op jit(solution)/shard_map/all_gather | solution.py:57
  119.8 12.7 %reshape.138 = bf16[128,32768]{1,0:T(8,128)(2,1)} reshape(bf16[32,4,32768]{2,1,0:T(4,128)(2,1)} %all-gather.3.cloned.1.call-done) | data formatting | bytes 16777216
  132.4 4.6 %convolution_convert_fusion = bf16[24,32768]{1,0:T(8,128)(2,1)S(1)} fusion(bf16[128,32768]{1,0:T(8,128)(2,1)} %reshape.138, s32[24]{0:T(128)S(1)} %get-tuple-element.23), kind=kOutput, calls=%fused_computation.2 | convolution fusion | flops 202116096 | bytes 9961568 | tf_op jit(solution)/shard_map/dot_general | solution.py:61
  140.2 3.0 fusion.44
  143.2 1.8 fusion.45
  145.1 3.1 %fusion.3 = bf16[768,1024]{1,0:T(8,128)(2,1)} fusion(f32[768,1024]{1,0:T(8,128)S(1)} %get-tuple-element.25, f32[24,32,1024]{2,1,0:T(8,128)S(1)} %copy-done.1, f32[768,1024]{1,0:T(8,128)S(1)} %fusion.45, bf16[768,1024]{1,0:T(8,128)(2,1)S(1)} %bitcast.71, bf16[1024,1024]{1,0:T(8,128)(2,1)S(1)} %convert_element_type.99), kind=kOutput, calls=%fused_computation.9 | convolution fusion | flops 1614544896 | bytes 14680064 | tf_op jit(solution)/shard_map/dot_general | solution.py:82
  148.1 2.7 reshape.113
  150.8 4.5 %convolution_convert_fusion.4 = bf16[768,1024]{1,0:T(8,128)(2,1)} fusion(bf16[768,1024]{1,0:T(8,128)(2,1)S(1)} %copy-done, bf16[1024,1024]{1,0:T(8,128)(2,1)} %convert_element_type.92), kind=kOutput, calls=%fused_computation.13 | convolution fusion | flops 1611399168 | bytes 5242880 | tf_op jit(solution)/shard_map/dot_general | solution.py:85
  155.4 2.6 reshape.110
  159.7 5.7 %all-to-all-start = ((f32[32,2,129]{2,1,0:T(2,128)}), f32[32,2,129]{2,1,0:T(2,128)S(1)}, u32[]{:S(2)}, u32[]{:S(2)}) async-start(f32[32,2,129]{2,1,0:T(2,128)} %pad_maximum_fusion.1), calls=%async_computation | async-start | bytes 131072 | tf_op jit(solution)/shard_map/all_to_all | solution.py:112
  165.4 2.0 fusion.4
  168.2 1.4 fusion.7
  169.5 6.3 %copy.46 = bf16[32,2,32768]{2,1,0:T(2,128)(2,1)} copy(bf16[32,2,32768]{2,0,1:T(8,128)(2,1)S(1)} %fusion.7) | data formatting | bytes 8388608 | tf_op jit(solution)/shard_map/dot_general | solution.py:116
  175.8 9.7 %all-to-all-start.1 = ((bf16[32,2,32768]{2,1,0:T(2,128)(2,1)}), bf16[32,2,32768]{2,1,0:T(2,128)(2,1)}, u32[]{:S(2)}, u32[]{:S(2)}) async-start(bf16[32,2,32768]{2,1,0:T(2,128)(2,1)} %copy.46), calls=%async_computation.1 | async-start | bytes 8388608 | tf_op jit(solution)/shard_map/all_to_all | solution.py:121
  186.4 95.0 %all-to-all-done.1 = bf16[32,2,32768]{2,1,0:T(2,128)(2,1)} async-done(((bf16[32,2,32768]{2,1,0:T(2,128)(2,1)}), bf16[32,2,32768]{2,1,0:T(2,128)(2,1)}, u32[]{:S(2)}, u32[]{:S(2)}) %all-to-all-start.1) | async-done | bytes 4194336 | tf_op jit(solution)/shard_map/all_to_all | solution.py:121
  281.4 7.3 %reshape.117 = bf16[64,32768]{1,0:T(8,128)(2,1)} reshape(bf16[32,2,32768]{2,1,0:T(2,128)(2,1)} %all-to-all-done.1) | data formatting | bytes 8388608 | tf_op jit(solution)/shard_map/reshape | solution.py:128
  288.7 3.6 %fusion.25 = f32[4,32768]{1,0:T(4,128)} fusion(bf16[64,32768]{1,0:T(8,128)(2,1)} %reshape.117, f32[64]{0:T(128)S(1)} %slice_reduce_fusion), kind=kOutput, calls=%fused_computation.49 | convolution fusion | flops 16777472 | bytes 4718848 | tf_op jit(solution)/shard_map/dot_general | solution.py:126
  (103 shorter events, 41.8 us)
Async XLA Ops:
  7.2 112.6 %all-gather.3.cloned.1.call-start = ((), (), s32[]{:S(2)}) async-start(), calls=%async_computation.2 | async-start | bytes 8650752 | tf_op jit(solution)/shard_map/all_gather | solution.py:57
  7.9 34.8 %collective-permute-start = (f32[1,32,1024]{2,1,0:T(8,128)}, f32[1,32,1024]{2,1,0:T(8,128)S(1)}, u32[]{:S(2)}, u32[]{:S(2)}) collective-permute-start(f32[1,32,1024]{2,1,0:T(8,128)} %param.6), channel_id=1, source_target_pairs={{32,0},{64,32},{96,64},{128,96},{160,128},{192,160},{224,192},{256... | collective-permute-start | bytes 393224 | tf_op jit(solution)/shard_map/ppermute | solution.py:12
  11.1 7.6 %copy-start.4 = (s32[24]{0:T(128)S(1)}, s32[24]{0:T(128)}, u32[]{:S(2)}) copy-start(s32[24]{0:T(128)} %param.9) | copy-start | bytes 292
  31.1 11.6 %copy-start.3 = (f32[1,32,1024]{2,1,0:T(8,128)S(1)}, f32[1,32,1024]{2,1,0:T(8,128)}, u32[]{:S(2)}) copy-start(f32[1,32,1024]{2,1,0:T(8,128)} %param.6) | copy-start | bytes 393220
  138.6 1.6 copy-start.2
  143.2 1.9 copy-start.1
  148.1 2.7 copy-start
  159.7 16.1 %all-to-all-start = ((f32[32,2,129]{2,1,0:T(2,128)}), f32[32,2,129]{2,1,0:T(2,128)S(1)}, u32[]{:S(2)}, u32[]{:S(2)}) async-start(f32[32,2,129]{2,1,0:T(2,128)} %pad_maximum_fusion.1), calls=%async_computation | async-start | bytes 131072 | tf_op jit(solution)/shard_map/all_to_all | solution.py:112
  175.8 105.6 %all-to-all-start.1 = ((bf16[32,2,32768]{2,1,0:T(2,128)(2,1)}), bf16[32,2,32768]{2,1,0:T(2,128)(2,1)}, u32[]{:S(2)}, u32[]{:S(2)}) async-start(bf16[32,2,32768]{2,1,0:T(2,128)(2,1)} %copy.46), calls=%async_computation.1 | async-start | bytes 8388608 | tf_op jit(solution)/shard_map/all_to_all | solution.py:121
Sparse Core Ops, SparseCore 0:
  11.1 108.5 all-gather.2
where the time goes:
time: 301 us; the launch traced here: 299 us
  waiting for transfers between devices  127 us (42%)
  local copies, waits for them, and re-layouts  104 us (35%)
  matrix products  27.1 us (9%)
  starting transfers between devices  15.4 us (5%)
  between operations  14.3 us (5%)
  other arithmetic  11.3 us (4%)
    all_to_all x1, waiting for transfers between devices, on_device(): lax.all_to_all(send_grad, 'dom', split_axis=0, concat_axis=0, tiled=True)  95 us
    gather x72, local copies, waits for them, and re-layouts  45.5 us
    all_gather x1, waiting for transfers between devices, on_device(): gathered_rows = lax.all_gather(owned_blips, 'dom', axis=0, tiled=True)  31.4 us
    unnamed x12, local copies, waits for them, and re-layouts  14.5 us
    convert_element_type x1, local copies, waits for them, and re-layouts, spline_tables(): plane_value.astype(jnp.bfloat16)  12.4 us
    convert_element_type x1, local copies, waits for them, and re-layouts, spline_tables(): plane_curve.astype(jnp.bfloat16)  11.4 us
    all_to_all x1, starting transfers between devices, on_device(): lax.all_to_all(send_grad, 'dom', split_axis=0, concat_axis=0, tiled=True)  9.69 us
    convert_element_type x1, other arithmetic, spline_tables(): plane_curve.astype(jnp.bfloat16)  7.56 us
  transfers between devices with their start and end apart: 4, of which 2 were waited for; matrix products, arithmetic and copies ran while one was open for 31% of the time, Pallas kernels for 0%

commit v1 on v0

--- a/solution.py
+++ b/solution.py
@@ -54,7 +54,16 @@
         1 - jnp.sum(place_hot.astype(jnp.int32), axis=1)
     )
     place_low = place_hot.astype(jnp.bfloat16)
-    gathered_rows = lax.all_gather(owned_blips, "dom", axis=0, tiled=True)
+    sites_open = lambda own_rows, axis_no: jnp.concatenate(
+        jax.lax.all_to_all(
+            jnp.stack([own_rows for _ in range(jax.lax.axis_size("dom"))], axis=0),
+            axis_name="dom",
+            split_axis=0,
+            concat_axis=0,
+        ),
+        axis_no,
+    )
+    gathered_rows = sites_open(owned_blips, 0)
     chosen = (
         target[:, None] == jnp.arange(gathered_rows.shape[0], dtype=jnp.int32)[None, :]
     ).astype(jnp.bfloat16)

time: 301 us -> 390 us (1.30)
  the two profiles are of different devices: /device:TPU:8 before, /device:TPU:1 now
where the time goes in v1:
time: 390 us; the launch traced here: 389 us
  waiting for transfers between devices  205 us (53%)
  local copies, waits for them, and re-layouts  112 us (29%)
  starting transfers between devices  34.8 us (9%)
  matrix products  27.1 us (7%)
  other arithmetic  8.69 us (2%)
    all_to_all x1, waiting for transfers between devices, on_device(): jax.lax.all_to_all(jnp.stack([own_rows for _ in range(jax.lax.axis_size('...  109 us
    all_to_all x1, waiting for transfers between devices, on_device(): lax.all_to_all(send_grad, 'dom', split_axis=0, concat_axis=0, tiled=True)  95.8 us
    gather x72, local copies, waits for them, and re-layouts  45.6 us
    all_to_all x1, starting transfers between devices, on_device(): jax.lax.all_to_all(jnp.stack([own_rows for _ in range(jax.lax.axis_size('...  14 us
    reshape x1, local copies, waits for them, and re-layouts, on_device(): jnp.concatenate(jax.lax.all_to_all(jnp.stack([own_rows for _ in range(jax...  12.7 us
    convert_element_type x1, local copies, waits for them, and re-layouts, spline_tables(): plane_value.astype(jnp.bfloat16)  12.4 us
    convert_element_type x1, local copies, waits for them, and re-layouts, spline_tables(): plane_curve.astype(jnp.bfloat16)  11.3 us
    all_to_all x1, starting transfers between devices, on_device(): lax.all_to_all(send_ham, 'dom', split_axis=0, concat_axis=0, tiled=True)  10.8 us
  transfers between devices with their start and end apart: 4, of which 2 were waited for; matrix products, arithmetic and copies ran while one was open for 23% of the time, Pallas kernels for 0%

profile of v1, /device:TPU:1, one launch (start us, length us, event | category | flops | bytes accessed | tf_op | source)
XLA Modules:
  0.0 388.6 jit_solution(1533134316209974466)
XLA Ops:
  0.6 7.9 %stack.2 = bf16[32,4,32768]{2,1,0:T(4,128)(2,1)} broadcast(bf16[4,32768]{1,0:T(4,128)(2,1)} %param.5), dimensions={1,2} | broadcast | bytes 8650752 | tf_op jit(solution)/shard_map/stack | solution.py:59
  8.6 14.0 %all-to-all-start = ((bf16[32,4,32768]{2,1,0:T(4,128)(2,1)}), bf16[32,4,32768]{2,1,0:T(4,128)(2,1)}, u32[]{:S(2)}, u32[]{:S(2)}) async-start(bf16[32,4,32768]{2,1,0:T(4,128)(2,1)} %stack.2), calls=%async_computation | async-start | bytes 16777216 | tf_op jit(solution)/shard_map/all_to_all | solution.py:58
  24.1 7.6 %fusion.1 = (bf16[32,32,32,32]{3,2,1,0:T(8,128)(2,1)}, bf16[32,32,32,32]{3,2,1,0:T(8,128)(2,1)}) fusion(f32[32,32]{1,0:T(8,128)S(1)} %copy.43, f32[32,32]{1,0:T(8,128)S(1)} %copy.40), kind=kLoop, calls=%fused_computation.6 | loop fusion | flops 6291456 | bytes 4202496 | tf_op jit(solution)/shard_map/convert_element_type | solution.py:32
  31.7 12.4 %convert_element_type.92 = bf16[1024,1024]{1,0:T(8,128)(2,1)} reshape(bf16[32,32,32,32]{3,2,1,0:T(8,128)(2,1)} %get-tuple-element.21) | data formatting | bytes 4194304 | tf_op jit(solution)/shard_map/convert_element_type | solution.py:31
  44.1 11.3 %convert_element_type.99 = bf16[1024,1024]{1,0:T(8,128)(2,1)S(1)} reshape(bf16[32,32,32,32]{3,2,1,0:T(8,128)(2,1)} %get-tuple-element.20) | data formatting | bytes 4194304 | tf_op jit(solution)/shard_map/convert_element_type | solution.py:32
  55.7 45.7 %while.1 = (s32[]{:T(128)}, f32[64,1024]{1,0:T(8,128)S(1)}, s32[24,2]{0,1:T(2,128)S(1)}, f32[24,32,1024]{2,1,0:T(8,128)}, s32[]{:T(128)}) while((s32[]{:T(128)}, f32[64,1024]{1,0:T(8,128)S(1)}, s32[24,2]{0,1:T(2,128)S(1)}, f32[24,32,1024]{2,1,0:T(8,128)}, s32[]{:T(128)}) %tuple.24), condition=%wide.while_cond, body=%wide.while_body.sunk | while | flops 2 | bytes 263257 | solution.py:77
  62.0 1.3 bitcast_dynamic-update-slice_fusion.2
  65.8 1.3 bitcast_dynamic-update-slice_fusion.2
  73.4 1.3 bitcast_dynamic-update-slice_fusion.2
  81.0 1.3 bitcast_dynamic-update-slice_fusion.2
  82.9 1.3 bitcast_dynamic-update-slice_fusion.2
  86.7 1.3 bitcast_dynamic-update-slice_fusion.2
  90.5 1.3 bitcast_dynamic-update-slice_fusion.2
  94.3 1.3 bitcast_dynamic-update-slice_fusion.2
  100.0 1.3 bitcast_dynamic-update-slice_fusion.2
  101.3 109.4 %all-to-all-done = bf16[32,4,32768]{2,1,0:T(4,128)(2,1)} async-done(((bf16[32,4,32768]{2,1,0:T(4,128)(2,1)}), bf16[32,4,32768]{2,1,0:T(4,128)(2,1)}, u32[]{:S(2)}, u32[]{:S(2)}) %all-to-all-start) | async-done | bytes 8388640 | tf_op jit(solution)/shard_map/all_to_all | solution.py:58
  210.7 12.7 %reshape.113 = bf16[128,32768]{1,0:T(8,128)(2,1)} reshape(bf16[32,4,32768]{2,1,0:T(4,128)(2,1)} %all-to-all-done) | data formatting | bytes 16777216 | tf_op jit(solution)/shard_map/reshape | solution.py:57
  223.4 4.6 %convolution_convert_fusion = bf16[24,32768]{1,0:T(8,128)(2,1)S(1)} fusion(bf16[128,32768]{1,0:T(8,128)(2,1)} %reshape.113, s32[24]{0:T(128)S(1)} %get-tuple-element.23), kind=kOutput, calls=%fused_computation.2 | convolution fusion | flops 202116096 | bytes 9961568 | tf_op jit(solution)/shard_map/dot_general | solution.py:70
  231.2 3.0 fusion.44
  234.1 1.8 fusion.45
  236.0 3.0 fusion.3
  239.1 2.7 reshape.119
  241.8 4.5 %convolution_convert_fusion.4 = bf16[768,1024]{1,0:T(8,128)(2,1)} fusion(bf16[768,1024]{1,0:T(8,128)(2,1)S(1)} %copy-done, bf16[1024,1024]{1,0:T(8,128)(2,1)} %convert_element_type.92), kind=kOutput, calls=%fused_computation.13 | convolution fusion | flops 1611399168 | bytes 5242880 | tf_op jit(solution)/shard_map/dot_general | solution.py:94
  246.3 2.6 reshape.116
  250.7 10.8 %all-to-all-start.1 = ((f32[32,2,129]{2,1,0:T(2,128)}), f32[32,2,129]{2,1,0:T(2,128)S(1)}, u32[]{:S(2)}, u32[]{:S(2)}) async-start(f32[32,2,129]{2,1,0:T(2,128)} %pad_maximum_fusion.1), calls=%async_computation.1 | async-start | bytes 131072 | tf_op jit(solution)/shard_map/all_to_all | solution.py:121
  261.5 2.0 fusion.4
  264.2 1.4 fusion.7
  265.6 6.3 %copy.46 = bf16[32,2,32768]{2,1,0:T(2,128)(2,1)} copy(bf16[32,2,32768]{2,0,1:T(8,128)(2,1)S(1)} %fusion.7) | data formatting | bytes 8388608 | tf_op jit(solution)/shard_map/dot_general | solution.py:125
  271.9 9.1 %all-to-all-start.2 = ((bf16[32,2,32768]{2,1,0:T(2,128)(2,1)}), bf16[32,2,32768]{2,1,0:T(2,128)(2,1)}, u32[]{:S(2)}, u32[]{:S(2)}) async-start(bf16[32,2,32768]{2,1,0:T(2,128)(2,1)} %copy.46), calls=%async_computation.2 | async-start | bytes 8388608 | tf_op jit(solution)/shard_map/all_to_all | solution.py:130
  281.9 95.8 %all-to-all-done.2 = bf16[32,2,32768]{2,1,0:T(2,128)(2,1)} async-done(((bf16[32,2,32768]{2,1,0:T(2,128)(2,1)}), bf16[32,2,32768]{2,1,0:T(2,128)(2,1)}, u32[]{:S(2)}, u32[]{:S(2)}) %all-to-all-start.2) | async-done | bytes 4194336 | tf_op jit(solution)/shard_map/all_to_all | solution.py:130
  377.7 7.3 %reshape.123 = bf16[64,32768]{1,0:T(8,128)(2,1)} reshape(bf16[32,2,32768]{2,1,0:T(2,128)(2,1)} %all-to-all-done.2) | data formatting | bytes 8388608 | tf_op jit(solution)/shard_map/reshape | solution.py:137
  385.0 3.6 fusion.25
  (107 shorter events, 42.1 us)
Async XLA Ops:
  8.6 14.0 %copy-start.3 = (f32[1,32,1024]{2,1,0:T(8,128)S(1)}, f32[1,32,1024]{2,1,0:T(8,128)}, u32[]{:S(2)}) copy-start(f32[1,32,1024]{2,1,0:T(8,128)} %param.6) | copy-start | bytes 393220
  8.6 15.1 %copy-start.4 = (s32[24,1]{0,1:T(1,128)S(1)}, s32[24,1]{0,1:T(1,128)}, u32[]{:S(2)}) copy-start(s32[24,1]{0,1:T(1,128)} %param.7) | copy-start | bytes 292
  8.6 15.4 %copy-start.5 = (s32[24]{0:T(128)S(1)}, s32[24]{0:T(128)}, u32[]{:S(2)}) copy-start(s32[24]{0:T(128)} %param.8) | copy-start | bytes 292
  8.6 202.2 %all-to-all-start = ((bf16[32,4,32768]{2,1,0:T(4,128)(2,1)}), bf16[32,4,32768]{2,1,0:T(4,128)(2,1)}, u32[]{:S(2)}, u32[]{:S(2)}) async-start(bf16[32,4,32768]{2,1,0:T(4,128)(2,1)} %stack.2), calls=%async_computation | async-start | bytes 16777216 | tf_op jit(solution)/shard_map/all_to_all | solution.py:58
  22.6 33.1 %collective-permute-start = (f32[1,32,1024]{2,1,0:T(8,128)S(1)}, f32[1,32,1024]{2,1,0:T(8,128)S(1)}, u32[]{:S(2)}, u32[]{:S(2)}) collective-permute-start(f32[1,32,1024]{2,1,0:T(8,128)S(1)} %copy-done.3), channel_id=1, source_target_pairs={{32,0},{64,32},{96,64},{128,96},{160,128},{192,160},{224,192},{256... | collective-permute-start | bytes 393224 | tf_op jit(solution)/shard_map/ppermute | solution.py:12
  24.1 7.6 %copy-start.6 = (s32[24]{0:T(128)S(1)}, s32[24]{0:T(128)}, u32[]{:S(2)}) copy-start(s32[24]{0:T(128)} %param.9) | copy-start | bytes 292
  229.6 1.6 copy-start.2
  234.1 1.9 copy-start.1
  239.1 2.7 copy-start
  250.7 21.2 %all-to-all-start.1 = ((f32[32,2,129]{2,1,0:T(2,128)}), f32[32,2,129]{2,1,0:T(2,128)S(1)}, u32[]{:S(2)}, u32[]{:S(2)}) async-start(f32[32,2,129]{2,1,0:T(2,128)} %pad_maximum_fusion.1), calls=%async_computation.1 | async-start | bytes 131072 | tf_op jit(solution)/shard_map/all_to_all | solution.py:121
  271.9 105.8 %all-to-all-start.2 = ((bf16[32,2,32768]{2,1,0:T(2,128)(2,1)}), bf16[32,2,32768]{2,1,0:T(2,128)(2,1)}, u32[]{:S(2)}, u32[]{:S(2)}) async-start(bf16[32,2,32768]{2,1,0:T(2,128)(2,1)} %copy.46), calls=%async_computation.2 | async-start | bytes 8388608 | tf_op jit(solution)/shard_map/all_to_all | solution.py:130
